TPU v7x, 32 devices: a whole 2x2x4 slice. The times are simulated.
32 devices in a mesh: wide: 8 (over y, x, core), narrow: 4 (over z).
Axes of the slice: x: 2, y: 2, z: 4, core: 2. Of those that a mesh axis runs over, the one named last changes fastest.
Arguments:
- tokens: bfloat16 [2048, 3072], P('wide'), may hold values from -6 to 6
- gain: bfloat16 [3072], replicated, may hold values from 0.5 to 1.5
- w_qkv: bfloat16 [3072, 3, 3072], P('wide', None, 'narrow'), may hold values from -0.109375 to 0.109375
- w_out: bfloat16 [3072, 3072], P('wide', 'narrow'), may hold values from -3 to 3
- cache: bfloat16 [256, 64, 2, 3072], P('wide', None, None, 'narrow'), may hold values from -104 to 104
- lengths: int32 [4], replicated, may hold values from 1 to 3584, as said below
- order: int32 [32], replicated, may hold values from 0 to 31, each once
- pages: int32 [256], replicated, may hold values from 0 to 255, each once
Outputs:
- mixed: bfloat16 [2048, 3072], P('wide', 'narrow')
Inputs may be any that keep to these rules, and one draw needn't show every extreme that they name: `lengths`: some request has exactly 3584 cached positions. `order`: each query block index once. `pages`: each cache block once.
All inputs are finite; a program needn't handle non-finite values.
Results may differ from a plain program's by a relative error of at most 0.02.
The roundings to bfloat16 on the way count: a program that leaves them out, or rounds other values in their place, can miss the bound.
Values may be sent and summed in bfloat16 or wider, within the bound.
No kernel may reach another device: no remote copies, remote signals or barrier semaphores. Data moves between devices by JAX's collectives and lax.ppermute only.
A program may use at most 192 MiB of HBM per device.

v0:
```python
import jax
import jax.numpy as jnp
from jax import lax
from jax.sharding import PartitionSpec as P

HD = 96
negative = -1e30
beyond = 1073741824


def rotate(values, positions):
    half_dim = values.shape[-1] // 2
    frequency = 10000.0 ** (-2.0 * jnp.arange(half_dim, dtype=jnp.float32) / values.shape[-1])
    angles = positions.astype(jnp.float32)[:, None] * frequency[None, :]
    cos_part = jnp.cos(angles)[:, None, :]
    sin_part = jnp.sin(angles)[:, None, :]
    lower_half = values[..., :half_dim]
    upper_half = values[..., half_dim:]
    return jnp.concatenate(
        [
            lower_half * cos_part - upper_half * sin_part,
            upper_half * cos_part + lower_half * sin_part,
        ],
        axis=-1,
    )


def lookup(small_table, key_index):
    matches = key_index[..., None] == jnp.arange(small_table.shape[0], dtype=jnp.int32)
    return jnp.sum(jnp.where(matches, small_table, 0), axis=-1)


def group_rows(onehot, terms, form):
    upper_part = terms.astype(jnp.bfloat16)
    lower_part = (terms - upper_part.astype(jnp.float32)).astype(jnp.bfloat16)
    first_sum = jnp.einsum(form, onehot, upper_part, preferred_element_type=jnp.float32)
    return first_sum + jnp.einsum(form, onehot, lower_part, preferred_element_type=jnp.float32)


def attend(chosen, key_rows, values, block_req, block_pos, query_pos, requests):
    score_scale = key_rows.shape[-1] ** (-0.5)
    scores = (
        jnp.einsum("lqhe,lkhe->lhqk", chosen, key_rows, preferred_element_type=jnp.float32)
        * score_scale
    )
    allowed = block_pos[:, None, None, :] <= query_pos[:, None, :, None]
    masked = jnp.where(allowed, scores, negative)
    block_max = jnp.max(masked, axis=3)
    owners = block_req[:, None] == jnp.arange(requests, dtype=jnp.int32)[None, :]
    dev_max = jnp.max(jnp.where(owners[:, :, None, None], block_max[:, None], negative), axis=0)
    local_max = dev_max[block_req]
    exp_terms = jnp.where(allowed, jnp.exp(masked - local_max[..., None]), 0.0)
    den_terms = jnp.sum(exp_terms, axis=3)
    weights = exp_terms.astype(jnp.bfloat16)
    num_terms = jnp.einsum("lhqk,lkhe->lqhe", weights, values, preferred_element_type=jnp.float32)
    onehot = owners.astype(jnp.bfloat16)
    dev_num = group_rows(onehot, num_terms, "lr,lqhe->rqhe")
    dev_den = group_rows(onehot, den_terms, "lr,lhq->rqh")
    return (jnp.transpose(dev_max, (0, 2, 1)), dev_num, dev_den)


def slice_head(array_in, head_idx):
    return lax.dynamic_slice_in_dim(array_in, head_idx, 1, 2)


def body(tokens, gain, w_qkv, w_out, cache, lengths, order, pages):
    wide_count = lax.axis_size("wide")
    wide_index = lax.axis_index("wide")
    tok_rows = tokens.shape[0]
    cache_count = cache.shape[0]
    blk_len = cache.shape[1]
    lane_width = cache.shape[3]
    head_count = lane_width // HD
    slot_count = tok_rows // blk_len
    block_total = order.shape[0]
    req_count = lengths.shape[0]
    per_request = block_total // req_count
    fresh_len = per_request * blk_len
    table_len = pages.shape[0] // req_count
    tok_float = tokens.astype(jnp.float32)
    inv_rms = lax.rsqrt(jnp.mean(tok_float * tok_float, axis=1, keepdims=True) + 1e-05)
    normed = (tok_float * inv_rms * gain.astype(jnp.float32)[None, :]).astype(jnp.bfloat16)
    part_in = lax.all_gather(w_qkv, "wide", axis=0, tiled=True)
    part_out = lax.all_gather(w_out, "wide", axis=0, tiled=True)
    acc_sum = jnp.einsum("tk,kcj->tcj", normed, part_in, preferred_element_type=jnp.float32)
    blk_idx = jnp.arange(blk_len, dtype=jnp.int32)
    slot_blocks = lax.dynamic_slice_in_dim(order, wide_index * slot_count, slot_count)
    slot_req = slot_blocks // per_request
    slot_start = lookup(lengths, slot_req) + slot_blocks % per_request * blk_len
    slot_pos = slot_start[:, None] + blk_idx[None, :]
    positions = slot_pos.reshape(tok_rows)
    queries = (
        rotate(acc_sum[:, 0].reshape(tok_rows, head_count, HD), positions)
        .astype(jnp.bfloat16)
        .reshape(tok_rows, lane_width)
    )
    keys_new = (
        rotate(acc_sum[:, 1].reshape(tok_rows, head_count, HD), positions)
        .astype(jnp.bfloat16)
        .reshape(slot_count, blk_len, head_count, HD)
    )
    vals_new = acc_sum[:, 2].astype(jnp.bfloat16).reshape(slot_count, blk_len, head_count, HD)
    all_queries = lax.all_gather(queries, "wide", axis=0, tiled=True)
    block_ids = jnp.arange(block_total, dtype=jnp.int32)
    slot_of = jnp.sum(
        jnp.where(order[None, :] == block_ids[:, None], block_ids[None, :], 0), axis=1
    )
    ordered = all_queries.reshape(block_total, blk_len, lane_width)[slot_of].reshape(
        req_count, fresh_len, head_count, HD
    )
    cache_ids = wide_index * cache_count + jnp.arange(cache_count, dtype=jnp.int32)
    page_ids = jnp.arange(pages.shape[0], dtype=jnp.int32)
    entries = jnp.sum(jnp.where(pages[None, :] == cache_ids[:, None], page_ids[None, :], 0), axis=1)
    cache_req = entries // table_len
    cache_pos = (entries % table_len)[:, None] * blk_len + blk_idx[None, :]
    cache_pos = jnp.where(cache_pos < lookup(lengths, cache_req)[:, None], cache_pos, beyond)
    block_req = jnp.concatenate([cache_req, slot_req])
    block_pos = jnp.concatenate([cache_pos, slot_pos])
    key_rows = jnp.concatenate(
        [cache[:, :, 0].reshape(cache_count, blk_len, head_count, HD), keys_new]
    )
    values = jnp.concatenate(
        [cache[:, :, 1].reshape(cache_count, blk_len, head_count, HD), vals_new]
    )
    chosen = ordered[block_req]
    query_pos = (
        lookup(lengths, block_req)[:, None] + jnp.arange(fresh_len, dtype=jnp.int32)[None, :]
    )

    def head_part(head_idx):
        return attend(
            slice_head(chosen, head_idx),
            slice_head(key_rows, head_idx),
            slice_head(values, head_idx),
            block_req,
            block_pos,
            query_pos,
            req_count,
        )

    head_max, head_num, head_den = lax.map(head_part, jnp.arange(head_count, dtype=jnp.int32))
    all_rows = req_count * fresh_len
    dev_max = jnp.transpose(head_max[..., 0], (1, 2, 0)).reshape(all_rows, head_count)
    dev_num = jnp.transpose(head_num[:, :, :, 0], (1, 2, 0, 3)).reshape(all_rows, head_count, HD)
    dev_den = jnp.transpose(head_den[..., 0], (1, 2, 0)).reshape(all_rows, head_count)
    sent_max = dev_max.reshape(wide_count, tok_rows, head_count)
    sent_num = dev_num.reshape(wide_count, tok_rows, lane_width)
    sent_den = dev_den.reshape(wide_count, tok_rows, head_count)
    got_max, got_num, got_den = (
        lax.all_to_all(sent_max, "wide", split_axis=0, concat_axis=0, tiled=True),
        lax.all_to_all(sent_num, "wide", split_axis=0, concat_axis=0, tiled=True),
        lax.all_to_all(sent_den, "wide", split_axis=0, concat_axis=0, tiled=True),
    )
    top_max = jnp.max(got_max, axis=0)
    factor = jnp.exp(got_max - top_max[None])
    num_own = jnp.sum(
        got_num.reshape(wide_count, tok_rows, head_count, HD) * factor[..., None], axis=0
    ).reshape(tok_rows, lane_width)
    den_own = jnp.sum(got_den * factor, axis=0)
    attention = (
        (num_own.reshape(tok_rows, head_count, HD) / den_own[..., None])
        .astype(jnp.bfloat16)
        .reshape(tok_rows, lane_width)
    )
    out_part = lax.dot_general(
        attention, part_out, (((1,), (1,)), ((), ())), preferred_element_type=jnp.float32
    )
    return lax.psum_scatter(
        out_part.astype(jnp.bfloat16), "narrow", scatter_dimension=1, tiled=True
    )


def solution(mesh):
    in_specs = (
        P("wide", None),
        P(),
        P("wide", None, "narrow"),
        P("wide", "narrow"),
        P("wide", None, None, "narrow"),
        P(),
        P(),
        P(),
    )
    out_specs = P("wide", "narrow")
    return jax.shard_map(body, mesh=mesh, in_specs=in_specs, out_specs=out_specs, check_vma=False)
```

profile of v0, /device:TPU:0, one launch (start us, length us, event | category | flops | bytes accessed | tf_op | source)
XLA Modules:
  0.0 541.1 jit_solution(3883787900699118251)
XLA Ops:
  11.8 78.9 %all-gather.4.cloned.1.call-done = bf16[3072,3,768]{2,0,1:T(8,128)(2,1)} async-done(((bf16[384,3,768]{2,0,1:T(8,128)(2,1)}), bf16[3072,3,768]{2,0,1:T(8,128)(2,1)}) %all-gather.4.cloned.1.call-update) | async-done | bytes 14155792 | tf_op jit(solution)/shard_map/all_gather | solution.py:83
  90.8 8.0 %fusion.53 = f32[256,3,768]{2,0,1:T(8,128)S(1)} fusion(bf16[3072,3,768]{2,0,1:T(8,128)(2,1)} %all-gather.4.cloned.1.call-done, bf16[256,3072]{1,0:T(8,128)(2,1)} %param.10, f32[3072]{0:T(1024)S(1)} %convert_element_type.74, f32[256]{0:T(256)S(1)} %add_rsqrt_fusion), kind=kOutput, calls=%fused_computation.67 | convolution fusion | flops 3627024384 | bytes 18101248 | tf_op jit(solution)/shard_map/tk,kcj->tcj/dot_general | solution.py:85
  103.9 31.1 %slice_reduce_fusion = (bf16[32,64,768]{2,1,0:T(8,128)(2,1)S(1)}, bf16[32,64,768]{2,1,0:T(8,128)(2,1)}) fusion(bf16[32,64,2,768]{3,2,1,0:T(2,128)(2,1)} %param.14), kind=kLoop, calls=%fused_computation.56 | loop fusion | bytes 12582912 | tf_op jit(solution)/shard_map/slice | solution.py:123
  135.0 8.2 %reshape_squeeze.13 = bf16[32,64,8,96]{3,2,1,0:T(8,128)(2,1)} reshape(bf16[32,64,768]{2,1,0:T(8,128)(2,1)} %get-tuple-element.148) | data formatting | bytes 6291456 | tf_op jit(solution)/shard_map/reshape;squeeze | solution.py:120
  143.2 5.4 reshape_squeeze.15
  151.5 3.4 maximum_maximum_fusion
  154.9 3.4 copy.75
  158.9 3.9 pad_maximum_fusion
  162.8 3.5 copy.76
  166.3 4.6 copy.69
  170.9 2.6 gather_fusion.1
  173.6 5.4 reshape.331
  179.0 5.8 %copy.70 = bf16[4,512,8,96]{1,3,2,0:T(8,128)(2,1)S(1)} copy(bf16[4,512,8,96]{3,2,1,0:T(8,128)(2,1)} %reshape.331) | data formatting | bytes 6291456 | tf_op jit(solution)/shard_map/reshape | solution.py:108
  184.8 11.3 %gather_fusion.2 = bf16[36,512,8,96]{1,3,2,0:T(8,128)(2,1)} fusion(bf16[4,512,8,96]{1,3,2,0:T(8,128)(2,1)S(1)} %copy.70, s32[1024]{0:T(1024)S(1)} %pad_clamp_fusion.1), kind=kCustom, calls=%fused_computation.2 | custom fusion | bytes 56623248 | tf_op jit(solution)/shard_map/gather | solution.py:125
  196.1 192.4 %while.15 = (s32[]{:T(128)}, f32[8,4,512,1]{2,0,1,3:T(8,128)}, f32[8,4,512,1,96]{2,1,4,3,0:T(4,128)}, f32[8,4,512,1]{2,0,1,3:T(8,128)S(1)}, s32[36]{0:T(128)S(1)...) while((s32[]{:T(128)}, f32[8,4,512,1]{2,0,1,3:T(8,128)}, ...), condition=%wide.region_10.11_spmd.clone, body=%wide.region_6.10_spmd.clone.sunk | while | flops 509732608 | bytes 71870680 | solution.py:141
  198.7 5.6 %fusion.92 = (f32[36,512]{1,0:T(8,128)S(1)}, f32[36,512,64]{1,2,0:T(8,128)}) fusion(s32[36,512]{1,0:T(8,128)S(1)} %iota_add_fusion.4, s32[36,64]{1,0:T(8,128)S(1)} %get-tuple-element.295, bf16[36,512,8,96]{1,3,2,0:T(8,128)(2,1)} %get-tuple-element.297, s32[]{:T(128)S(6)} %select_n.201, bf16[36,64,8,96]{3,1,0,2:T(8,128)(2,1)} %get-tuple-element.298), kind=kOutput, calls=%fused_computation.13.clone.1 | convolution fusion | flops 231192576 | bytes 9005056 | tf_op jit(solution)/shard_map/while/body/eval_jaxpr/lqhe,lkhe->lhqk/dot_general | solution.py:43
  206.7 4.1 fusion.94
  214.9 3.3 fusion.98
  222.8 5.6 %fusion.92 = (f32[36,512]{1,0:T(8,128)S(1)}, f32[36,512,64]{1,2,0:T(8,128)}) fusion(s32[36,512]{1,0:T(8,128)S(1)} %iota_add_fusion.4, s32[36,64]{1,0:T(8,128)S(1)} %get-tuple-element.295, bf16[36,512,8,96]{1,3,2,0:T(8,128)(2,1)} %get-tuple-element.297, s32[]{:T(128)S(6)} %select_n.201, bf16[36,64,8,96]{3,1,0,2:T(8,128)(2,1)} %get-tuple-element.298), kind=kOutput, calls=%fused_computation.13.clone.1 | convolution fusion | flops 231192576 | bytes 9005056 | tf_op jit(solution)/shard_map/while/body/eval_jaxpr/lqhe,lkhe->lhqk/dot_general | solution.py:43
  230.8 4.1 fusion.94
  238.9 3.3 fusion.98
  246.8 5.6 %fusion.92 = (f32[36,512]{1,0:T(8,128)S(1)}, f32[36,512,64]{1,2,0:T(8,128)}) fusion(s32[36,512]{1,0:T(8,128)S(1)} %iota_add_fusion.4, s32[36,64]{1,0:T(8,128)S(1)} %get-tuple-element.295, bf16[36,512,8,96]{1,3,2,0:T(8,128)(2,1)} %get-tuple-element.297, s32[]{:T(128)S(6)} %select_n.201, bf16[36,64,8,96]{3,1,0,2:T(8,128)(2,1)} %get-tuple-element.298), kind=kOutput, calls=%fused_computation.13.clone.1 | convolution fusion | flops 231192576 | bytes 9005056 | tf_op jit(solution)/shard_map/while/body/eval_jaxpr/lqhe,lkhe->lhqk/dot_general | solution.py:43
  254.8 4.1 fusion.94
  263.0 3.4 fusion.98
  270.9 5.6 %fusion.92 = (f32[36,512]{1,0:T(8,128)S(1)}, f32[36,512,64]{1,2,0:T(8,128)}) fusion(s32[36,512]{1,0:T(8,128)S(1)} %iota_add_fusion.4, s32[36,64]{1,0:T(8,128)S(1)} %get-tuple-element.295, bf16[36,512,8,96]{1,3,2,0:T(8,128)(2,1)} %get-tuple-element.297, s32[]{:T(128)S(6)} %select_n.201, bf16[36,64,8,96]{3,1,0,2:T(8,128)(2,1)} %get-tuple-element.298), kind=kOutput, calls=%fused_computation.13.clone.1 | convolution fusion | flops 231192576 | bytes 9005056 | tf_op jit(solution)/shard_map/while/body/eval_jaxpr/lqhe,lkhe->lhqk/dot_general | solution.py:43
  278.9 4.1 fusion.94
  287.1 3.3 fusion.98
  295.0 5.6 %fusion.92 = (f32[36,512]{1,0:T(8,128)S(1)}, f32[36,512,64]{1,2,0:T(8,128)}) fusion(s32[36,512]{1,0:T(8,128)S(1)} %iota_add_fusion.4, s32[36,64]{1,0:T(8,128)S(1)} %get-tuple-element.295, bf16[36,512,8,96]{1,3,2,0:T(8,128)(2,1)} %get-tuple-element.297, s32[]{:T(128)S(6)} %select_n.201, bf16[36,64,8,96]{3,1,0,2:T(8,128)(2,1)} %get-tuple-element.298), kind=kOutput, calls=%fused_computation.13.clone.1 | convolution fusion | flops 231192576 | bytes 9005056 | tf_op jit(solution)/shard_map/while/body/eval_jaxpr/lqhe,lkhe->lhqk/dot_general | solution.py:43
  303.0 4.1 fusion.94
  311.2 3.3 fusion.98
  319.0 5.6 %fusion.92 = (f32[36,512]{1,0:T(8,128)S(1)}, f32[36,512,64]{1,2,0:T(8,128)}) fusion(s32[36,512]{1,0:T(8,128)S(1)} %iota_add_fusion.4, s32[36,64]{1,0:T(8,128)S(1)} %get-tuple-element.295, bf16[36,512,8,96]{1,3,2,0:T(8,128)(2,1)} %get-tuple-element.297, s32[]{:T(128)S(6)} %select_n.201, bf16[36,64,8,96]{3,1,0,2:T(8,128)(2,1)} %get-tuple-element.298), kind=kOutput, calls=%fused_computation.13.clone.1 | convolution fusion | flops 231192576 | bytes 9005056 | tf_op jit(solution)/shard_map/while/body/eval_jaxpr/lqhe,lkhe->lhqk/dot_general | solution.py:43
  327.0 4.1 fusion.94
  335.2 3.3 fusion.98
  343.1 5.6 %fusion.92 = (f32[36,512]{1,0:T(8,128)S(1)}, f32[36,512,64]{1,2,0:T(8,128)}) fusion(s32[36,512]{1,0:T(8,128)S(1)} %iota_add_fusion.4, s32[36,64]{1,0:T(8,128)S(1)} %get-tuple-element.295, bf16[36,512,8,96]{1,3,2,0:T(8,128)(2,1)} %get-tuple-element.297, s32[]{:T(128)S(6)} %select_n.201, bf16[36,64,8,96]{3,1,0,2:T(8,128)(2,1)} %get-tuple-element.298), kind=kOutput, calls=%fused_computation.13.clone.1 | convolution fusion | flops 231192576 | bytes 9005056 | tf_op jit(solution)/shard_map/while/body/eval_jaxpr/lqhe,lkhe->lhqk/dot_general | solution.py:43
  351.1 4.1 fusion.94
  359.3 3.3 fusion.98
  367.1 5.6 %fusion.92 = (f32[36,512]{1,0:T(8,128)S(1)}, f32[36,512,64]{1,2,0:T(8,128)}) fusion(s32[36,512]{1,0:T(8,128)S(1)} %iota_add_fusion.4, s32[36,64]{1,0:T(8,128)S(1)} %get-tuple-element.295, bf16[36,512,8,96]{1,3,2,0:T(8,128)(2,1)} %get-tuple-element.297, s32[]{:T(128)S(6)} %select_n.201, bf16[36,64,8,96]{3,1,0,2:T(8,128)(2,1)} %get-tuple-element.298), kind=kOutput, calls=%fused_computation.13.clone.1 | convolution fusion | flops 231192576 | bytes 9005056 | tf_op jit(solution)/shard_map/while/body/eval_jaxpr/lqhe,lkhe->lhqk/dot_general | solution.py:43
  375.1 4.1 fusion.94
  383.3 3.3 fusion.98
  388.6 7.7 %all_to_all.15 = f32[8,256,8]{1,2,0:T(8,128)S(1)} all-to-all(f32[8,256,8]{1,2,0:T(8,128)S(1)} %bitcast.138), channel_id=1, replica_groups=mesh['wide'=8,'narrow'=4] {'wide'}, dimensions={0} | all-to-all | bytes 131072 | tf_op jit(solution)/shard_map/all_to_all | solution.py:152
  396.2 3.6 all-to-all-start.1
  399.9 7.9 %reshape_reshape.9 = f32[8,256,768]{1,0,2:T(8,128)} reshape(f32[4,512,8,96]{1,0,3,2:T(4,128)} %bitcast.132) | data formatting | bytes 12582912 | tf_op jit(solution)/shard_map/reshape;reshape | solution.py:147
  407.7 7.5 %copy.77 = f32[8,256,768]{1,2,0:T(8,128)} copy(f32[8,256,768]{1,0,2:T(8,128)} %reshape_reshape.9) | data formatting | bytes 12582912 | tf_op jit(solution)/shard_map/reshape;reshape | solution.py:147
  415.2 4.8 all-to-all-start
  420.0 71.5 %all-to-all-done = f32[8,256,768]{1,2,0:T(8,128)} async-done(((f32[8,256,768]{1,2,0:T(8,128)}), f32[8,256,768]{1,2,0:T(8,128)}, u32[]{:S(2)}, u32[]{:S(2)}) %all-to-all-start) | async-done | bytes 6291488 | tf_op jit(solution)/shard_map/all_to_all | solution.py:151
  491.5 3.4 fusion.48
  495.0 4.9 convolution_convert_fusion
  500.0 34.6 %reduce-scatter.2.cloned.1.call-done = bf16[256,768]{1,0:T(8,128)(2,1)} async-done(((bf16[256,3072]{1,0:T(8,128)(2,1)}), bf16[256,768]{1,0:T(8,128)(2,1)}) %reduce-scatter.2.cloned.1.call-update) | async-done | bytes 393232 | tf_op jit(solution)/shard_map/reduce_scatter | solution.py:168
  (242 shorter events, 86.0 us)
Async XLA Ops:
  6.5 84.2 %all-gather.4.cloned.1.call-start = ((), (), s32[]{:S(2)}) async-start(), calls=%async_computation.4 | async-start | bytes 15925248 | tf_op jit(solution)/shard_map/all_gather | solution.py:83
  7.3 159.0 %all-gather.6.cloned.1.call-start = ((), (), s32[]{:S(2)}) async-start(), calls=%async_computation.5 | async-start | bytes 3538944 | tf_op jit(solution)/shard_map/all_gather | solution.py:103
  98.8 1.5 copy-start
  98.8 4.5 copy-start.1
  98.8 4.8 copy-start.3
  98.8 4.9 copy-start.2
  102.5 392.5 %all-gather.8.cloned.1.call-start = ((), (), s32[]{:S(2)}) async-start(), calls=%async_computation.6 | async-start | bytes 5308416 | tf_op jit(solution)/shard_map/all_gather | solution.py:84
  212.0 6.3 %slice-start = ((s8[4718592]{0:T(1024)(128)(4,1)}), s8[4194304]{0:T(1024)(128)(4,1)S(1)}, s32[]{:S(2)}) async-start(s8[4718592]{0:T(1024)(128)(4,1)} %bitcast.129), calls=%async_computation.8 | async-start | bytes 8388608 | tf_op jit(solution)/shard_map/while
  214.4 3.9 slice-start.1
  236.0 6.3 %slice-start = ((s8[4718592]{0:T(1024)(128)(4,1)}), s8[4194304]{0:T(1024)(128)(4,1)S(1)}, s32[]{:S(2)}) async-start(s8[4718592]{0:T(1024)(128)(4,1)} %bitcast.129), calls=%async_computation.8 | async-start | bytes 8388608 | tf_op jit(solution)/shard_map/while
  238.4 3.9 slice-start.1
  260.1 6.3 %slice-start = ((s8[4718592]{0:T(1024)(128)(4,1)}), s8[4194304]{0:T(1024)(128)(4,1)S(1)}, s32[]{:S(2)}) async-start(s8[4718592]{0:T(1024)(128)(4,1)} %bitcast.129), calls=%async_computation.8 | async-start | bytes 8388608 | tf_op jit(solution)/shard_map/while
  262.5 3.9 slice-start.1
  284.2 6.3 %slice-start = ((s8[4718592]{0:T(1024)(128)(4,1)}), s8[4194304]{0:T(1024)(128)(4,1)S(1)}, s32[]{:S(2)}) async-start(s8[4718592]{0:T(1024)(128)(4,1)} %bitcast.129), calls=%async_computation.8 | async-start | bytes 8388608 | tf_op jit(solution)/shard_map/while
  286.6 3.9 slice-start.1
  308.2 6.3 %slice-start = ((s8[4718592]{0:T(1024)(128)(4,1)}), s8[4194304]{0:T(1024)(128)(4,1)S(1)}, s32[]{:S(2)}) async-start(s8[4718592]{0:T(1024)(128)(4,1)} %bitcast.129), calls=%async_computation.8 | async-start | bytes 8388608 | tf_op jit(solution)/shard_map/while
  310.6 3.9 slice-start.1
  332.2 6.3 %slice-start = ((s8[4718592]{0:T(1024)(128)(4,1)}), s8[4194304]{0:T(1024)(128)(4,1)S(1)}, s32[]{:S(2)}) async-start(s8[4718592]{0:T(1024)(128)(4,1)} %bitcast.129), calls=%async_computation.8 | async-start | bytes 8388608 | tf_op jit(solution)/shard_map/while
  334.7 3.9 slice-start.1
  356.3 6.3 %slice-start = ((s8[4718592]{0:T(1024)(128)(4,1)}), s8[4194304]{0:T(1024)(128)(4,1)S(1)}, s32[]{:S(2)}) async-start(s8[4718592]{0:T(1024)(128)(4,1)} %bitcast.129), calls=%async_computation.8 | async-start | bytes 8388608 | tf_op jit(solution)/shard_map/while
  358.7 3.9 slice-start.1
  380.4 6.3 %slice-start = ((s8[4718592]{0:T(1024)(128)(4,1)}), s8[4194304]{0:T(1024)(128)(4,1)S(1)}, s32[]{:S(2)}) async-start(s8[4718592]{0:T(1024)(128)(4,1)} %bitcast.129), calls=%async_computation.8 | async-start | bytes 8388608 | tf_op jit(solution)/shard_map/while
  382.8 3.9 slice-start.1
  396.2 18.9 %all-to-all-start.1 = ((f32[8,256,8]{1,2,0:T(8,128)}), f32[8,256,8]{1,2,0:T(8,128)S(1)}, u32[]{:S(2)}, u32[]{:S(2)}) async-start(f32[8,256,8]{1,2,0:T(8,128)} %bitcast.16), calls=%async_computation.1 | async-start | bytes 131072 | tf_op jit(solution)/shard_map/all_to_all | solution.py:150
  415.2 76.4 %all-to-all-start = ((f32[8,256,768]{1,2,0:T(8,128)}), f32[8,256,768]{1,2,0:T(8,128)}, u32[]{:S(2)}, u32[]{:S(2)}) async-start(f32[8,256,768]{1,2,0:T(8,128)} %copy.77), calls=%async_computation | async-start | bytes 12582912 | tf_op jit(solution)/shard_map/all_to_all | solution.py:151
  419.9 114.6 %reduce-scatter.2.cloned.1.call-start = ((), (), s32[]{:S(2)}) async-start(), calls=%async_computation.7 | async-start | bytes 1966080 | tf_op jit(solution)/shard_map/reduce_scatter | solution.py:168
Sparse Core Ops, SparseCore 0:
  9.3 81.4 all-gather.3
  102.6 32.8 all-gather.5
  137.4 38.9 all-gather.7
  500.1 34.4 reduce-scatter.1
where the time goes:
time: 543 us; the launch traced here: 541 us
  waiting for transfers between devices  186 us (34%)
  matrix products  138 us (25%)
  local copies, waits for them, and re-layouts  125 us (23%)
  other arithmetic  45.2 us (8%)
  loops' own time  16.2 us (3%)
  between operations  13.4 us (2%)
  starting transfers between devices  8.49 us (2%)
  blocking collectives  7.68 us (1%)
    all_gather x1, waiting for transfers between devices, body(): part_in = lax.all_gather(w_qkv, 'wide', axis=0, tiled=True)  78.9 us
    all_to_all x1, waiting for transfers between devices, body(): lax.all_to_all(sent_num, 'wide', split_axis=0, concat_axis=0, tiled=True)  71.5 us
    dot_general x8, matrix products, attend(): jnp.einsum('lqhe,lkhe->lhqk', chosen, key_rows, preferred_element_type=jn...  44.8 us
    reduce_scatter x1, waiting for transfers between devices, body(): lax.psum_scatter(out_part.astype(jnp.bfloat16), 'narrow', scatter_dimensi...  34.6 us
    dot_general x8, matrix products, attend(): jnp.einsum('lhqk,lkhe->lqhe', weights, values, preferred_element_type=jnp...  32.7 us
    slice x1, local copies, waits for them, and re-layouts, body(): cache[:, :, 1].reshape(cache_count, blk_len, head_count, HD)  31.1 us
    dot_general x16, matrix products, group_rows(): jnp.einsum(form, onehot, upper_part, preferred_element_type=jnp.float32)  27.6 us
    dot_general x16, matrix products, group_rows(): jnp.einsum(form, onehot, lower_part, preferred_element_type=jnp.float32)  20.2 us
  transfers between devices with their start and end apart: 6, of which 3 were waited for; matrix products, arithmetic and copies ran while one was open for 54% of the time, Pallas kernels for 0%

commit v1 on v0

--- a/solution.py
+++ b/solution.py
@@ -6,6 +6,22 @@
 HD = 96
 negative = -1e30
 beyond = 1073741824
+
+
+def product_in_turn(x, axis, dim, term):
+    devices, place, rows = (lax.axis_size(axis), lax.axis_index(axis), x.shape[dim])
+    ahead = [(i, (i + 1) % devices) for i in range(devices)]
+    backward = [(i, (i - 1) % devices) for i in range(devices)]
+    halfway = devices // 2
+    from_left = from_right = x
+    subtotal = term(x, place * rows)
+    for hop in range(1, halfway + 1):
+        from_left = lax.ppermute(from_left, axis, ahead)
+        if hop < devices - halfway:
+            from_right = lax.ppermute(from_right, axis, backward)
+            subtotal = subtotal + term(from_right, (place + hop) % devices * rows)
+        subtotal = subtotal + term(from_left, (place - hop) % devices * rows)
+    return subtotal
 
 
 def rotate(values, positions):
@@ -80,9 +96,18 @@
     tok_float = tokens.astype(jnp.float32)
     inv_rms = lax.rsqrt(jnp.mean(tok_float * tok_float, axis=1, keepdims=True) + 1e-05)
     normed = (tok_float * inv_rms * gain.astype(jnp.float32)[None, :]).astype(jnp.bfloat16)
-    part_in = lax.all_gather(w_qkv, "wide", axis=0, tiled=True)
     part_out = lax.all_gather(w_out, "wide", axis=0, tiled=True)
-    acc_sum = jnp.einsum("tk,kcj->tcj", normed, part_in, preferred_element_type=jnp.float32)
+    acc_sum = product_in_turn(
+        w_qkv,
+        "wide",
+        0,
+        lambda part, at: jnp.einsum(
+            "tk,kcj->tcj",
+            lax.dynamic_slice_in_dim(normed, at, part.shape[0], axis=1),
+            part,
+            preferred_element_type=jnp.float32,
+        ),
+    )
     blk_idx = jnp.arange(blk_len, dtype=jnp.int32)
     slot_blocks = lax.dynamic_slice_in_dim(order, wide_index * slot_count, slot_count)
     slot_req = slot_blocks // per_request

time: 543 us -> 605 us (1.11); the launches traced: 541 us -> 596 us
  waiting for transfers between devices: 186 us -> 216 us
  starting transfers between devices: 8.49 us -> 18.9 us
    ppermute x0 -> x7, waiting for transfers between devices: none -> 108 us  [the longest x4 108 us: product_in_turn(): from_left = lax.ppermute(from_left, axis, ahead)]
    all_gather x1 -> x0, waiting for transfers between devices: 78.9 us -> none  [body(): part_in = lax.all_gather(w_qkv, 'wide', axis=0, tiled=True)]
    ppermute x0 -> x7, starting transfers between devices: none -> 10.5 us  [the longest x3 6.01 us: product_in_turn(): from_right = lax.ppermute(from_right, axis, backward)]
    dot_general x1 -> x8, matrix products: 7.98 us -> 12.4 us  [body(): jnp.einsum('tk,kcj->tcj', lax.dynamic_slice_in_dim(normed, at, part.shape...]
  transfers between devices with their start and end apart: 6 -> 12, of which waited for: 3 -> 6; matrix products, arithmetic and copies ran while one was open for 54% -> 52% of each run, Pallas kernels for 0% -> 0%
where the time goes in v1:
time: 605 us; the launch traced here: 596 us
  waiting for transfers between devices  216 us (36%)
  matrix products  143 us (24%)
  local copies, waits for them, and re-layouts  128 us (21%)
  other arithmetic  48 us (8%)
  starting transfers between devices  18.9 us (3%)
  loops' own time  16.2 us (3%)
  between operations  13.7 us (2%)
  blocking collectives  12.4 us (2%)
    ppermute x4, waiting for transfers between devices, product_in_turn(): from_left = lax.ppermute(from_left, axis, ahead)  108 us
    all_to_all x1, waiting for transfers between devices, body(): lax.all_to_all(sent_num, 'wide', split_axis=0, concat_axis=0, tiled=True)  71.5 us
    dot_general x8, matrix products, attend(): jnp.einsum('lqhe,lkhe->lhqk', chosen, key_rows, preferred_element_type=jn...  44.8 us
    reduce_scatter x1, waiting for transfers between devices, body(): lax.psum_scatter(out_part.astype(jnp.bfloat16), 'narrow', scatter_dimensi...  36.6 us
    dot_general x8, matrix products, attend(): jnp.einsum('lhqk,lkhe->lqhe', weights, values, preferred_element_type=jnp...  32.8 us
    slice x1, local copies, waits for them, and re-layouts, body(): cache[:, :, 1].reshape(cache_count, blk_len, head_count, HD)  31.4 us
    dot_general x16, matrix products, group_rows(): jnp.einsum(form, onehot, upper_part, preferred_element_type=jnp.float32)  27.6 us
    dot_general x16, matrix products, group_rows(): jnp.einsum(form, onehot, lower_part, preferred_element_type=jnp.float32)  20.2 us
  transfers between devices with their start and end apart: 12, of which 6 were waited for; matrix products, arithmetic and copies ran while one was open for 52% of the time, Pallas kernels for 0%

profile of v1, /device:TPU:0, one launch (start us, length us, event | category | flops | bytes accessed | tf_op | source)
XLA Modules:
  0.0 595.8 jit_solution(8342758159301795644)
XLA Ops:
  9.9 36.8 %collective-permute-done.1 = bf16[384,3,768]{2,0,1:T(8,128)(2,1)S(1)} collective-permute-done((bf16[384,3,768]{2,0,1:T(8,128)(2,1)}, bf16[384,3,768]{2,0,1:T(8,128)(2,1)S(1)}, u32[]{:S(2)}, u32[]{:S(2)}) %collective-permute-start.1) | collective-permute-done | bytes 1769504 | tf_op jit(solution)/shard_map/ppermute | solution.py:19
  51.7 32.6 %collective-permute-done.3 = bf16[384,3,768]{2,0,1:T(8,128)(2,1)} collective-permute-done((bf16[384,3,768]{2,0,1:T(8,128)(2,1)S(1)}, bf16[384,3,768]{2,0,1:T(8,128)(2,1)}, u32[]{:S(2)}, u32[]{:S(2)}) %collective-permute-start.3) | collective-permute-done | bytes 1769504 | tf_op jit(solution)/shard_map/ppermute | solution.py:19
  94.9 24.3 %collective-permute-done.5 = bf16[384,3,768]{2,0,1:T(8,128)(2,1)} collective-permute-done((bf16[384,3,768]{2,0,1:T(8,128)(2,1)}, bf16[384,3,768]{2,0,1:T(8,128)(2,1)}, u32[]{:S(2)}, u32[]{:S(2)}) %collective-permute-start.5) | collective-permute-done | bytes 1769504 | tf_op jit(solution)/shard_map/ppermute | solution.py:19
  131.5 13.9 %collective-permute-done.6 = bf16[384,3,768]{2,0,1:T(8,128)(2,1)S(1)} collective-permute-done((bf16[384,3,768]{2,0,1:T(8,128)(2,1)}, bf16[384,3,768]{2,0,1:T(8,128)(2,1)S(1)}, u32[]{:S(2)}, u32[]{:S(2)}) %collective-permute-start.6) | collective-permute-done | bytes 1769504 | tf_op jit(solution)/shard_map/ppermute | solution.py:19
  152.0 31.4 %slice_reduce_fusion = (bf16[32,64,768]{2,1,0:T(8,128)(2,1)S(1)}, bf16[32,64,768]{2,1,0:T(8,128)(2,1)}) fusion(bf16[32,64,2,768]{3,2,1,0:T(2,128)(2,1)} %param.14), kind=kLoop, calls=%fused_computation.56 | loop fusion | bytes 12582912 | tf_op jit(solution)/shard_map/slice | solution.py:148
  183.3 8.3 %reshape_squeeze.13 = bf16[32,64,8,96]{3,2,1,0:T(8,128)(2,1)} reshape(bf16[32,64,768]{2,1,0:T(8,128)(2,1)} %get-tuple-element.148) | data formatting | bytes 6291456 | tf_op jit(solution)/shard_map/reshape;squeeze | solution.py:145
  191.6 5.4 reshape_squeeze.15
  200.0 3.4 maximum_maximum_fusion
  203.4 3.4 copy.75
  210.5 3.5 copy.76
  214.0 4.8 copy.69
  221.4 5.4 reshape.331
  226.8 5.8 copy.70
  232.6 11.3 %gather_fusion.2 = bf16[36,512,8,96]{1,3,2,0:T(8,128)(2,1)} fusion(bf16[4,512,8,96]{1,3,2,0:T(8,128)(2,1)S(1)} %copy.70, s32[1024]{0:T(1024)S(1)} %pad_clamp_fusion.1), kind=kCustom, calls=%fused_computation.2 | custom fusion | bytes 56623248 | tf_op jit(solution)/shard_map/gather | solution.py:150
  243.9 192.5 %while.15 = (s32[]{:T(128)}, f32[8,4,512,1]{2,0,1,3:T(8,128)}, f32[8,4,512,1,96]{2,1,4,3,0:T(4,128)}, f32[8,4,512,1]{2,0,1,3:T(8,128)S(1)}, s32[36]{0:T(128)S(1)...) while((s32[]{:T(128)}, f32[8,4,512,1]{2,0,1,3:T(8,128)}, ...), condition=%wide.region_10.11_spmd.clone, body=%wide.region_6.10_spmd.clone.sunk | while | flops 509732608 | bytes 71870680 | solution.py:166
  246.5 5.6 fusion.125
  254.5 4.1 fusion.127
  262.7 3.3 fusion.131
  270.6 5.6 fusion.125
  278.6 4.1 fusion.127
  286.8 3.3 fusion.131
  294.6 5.6 fusion.125
  302.6 4.1 fusion.127
  310.8 3.4 fusion.131
  318.7 5.6 fusion.125
  326.7 4.1 fusion.127
  334.9 3.3 fusion.131
  342.8 5.6 fusion.125
  350.8 4.1 fusion.127
  359.0 3.3 fusion.131
  366.8 5.6 fusion.125
  374.8 4.1 fusion.127
  383.0 3.3 fusion.131
  390.9 5.6 fusion.125
  398.9 4.1 fusion.127
  407.1 3.3 fusion.131
  414.9 5.6 fusion.125
  422.9 4.1 fusion.127
  431.1 3.3 fusion.131
  436.4 12.4 %all_to_all.15 = f32[8,256,8]{1,2,0:T(8,128)S(1)} all-to-all(f32[8,256,8]{1,2,0:T(8,128)S(1)} %bitcast.166), channel_id=1, replica_groups=mesh['wide'=8,'narrow'=4] {'wide'}, dimensions={0} | all-to-all | bytes 131072 | tf_op jit(solution)/shard_map/all_to_all | solution.py:177
  448.7 3.6 all-to-all-start.1
  452.3 7.9 %reshape_reshape.9 = f32[8,256,768]{1,0,2:T(8,128)} reshape(f32[4,512,8,96]{1,0,3,2:T(4,128)} %bitcast.160) | data formatting | bytes 12582912 | tf_op jit(solution)/shard_map/reshape;reshape | solution.py:172
  460.2 7.5 %copy.77 = f32[8,256,768]{1,2,0:T(8,128)} copy(f32[8,256,768]{1,0,2:T(8,128)} %reshape_reshape.9) | data formatting | bytes 12582912 | tf_op jit(solution)/shard_map/reshape;reshape | solution.py:172
  467.7 4.7 all-to-all-start
  472.5 71.5 %all-to-all-done = f32[8,256,768]{1,2,0:T(8,128)} async-done(((f32[8,256,768]{1,2,0:T(8,128)}), f32[8,256,768]{1,2,0:T(8,128)}, u32[]{:S(2)}, u32[]{:S(2)}) %all-to-all-start) | async-done | bytes 6291488 | tf_op jit(solution)/shard_map/all_to_all | solution.py:176
  544.0 3.4 fusion.48
  547.5 4.9 convolution_convert_fusion
  552.4 36.6 %reduce-scatter.2.cloned.1.call-done = bf16[256,768]{1,0:T(8,128)(2,1)} async-done(((bf16[256,3072]{1,0:T(8,128)(2,1)}), bf16[256,768]{1,0:T(8,128)(2,1)}) %reduce-scatter.2.cloned.1.call-update) | async-done | bytes 393232 | tf_op jit(solution)/shard_map/reduce_scatter | solution.py:193
  (275 shorter events, 119.2 us)
Async XLA Ops:
  6.5 85.6 %copy-start.1 = (bf16[384,3,768]{2,0,1:T(8,128)(2,1)S(1)}, bf16[384,3,768]{2,0,1:T(8,128)(2,1)}, u32[]{:S(2)}) copy-start(bf16[384,3,768]{2,0,1:T(8,128)(2,1)} %param.12) | copy-start | bytes 5308420
  6.5 207.5 %all-gather.3.cloned.1.call-start = ((), (), s32[]{:S(2)}) async-start(), calls=%async_computation.4 | async-start | bytes 3538944 | tf_op jit(solution)/shard_map/all_gather | solution.py:128
  6.5 40.2 %collective-permute-start.1 = (bf16[384,3,768]{2,0,1:T(8,128)(2,1)}, bf16[384,3,768]{2,0,1:T(8,128)(2,1)S(1)}, u32[]{:S(2)}, u32[]{:S(2)}) collective-permute-start(bf16[384,3,768]{2,0,1:T(8,128)(2,1)} %param.12), channel_id=1, source_target_pairs={{0,4},{4,8},{8,12},{12,16},{16,20},{20,24},{24,28},{28,0},{1,5},{5... | collective-permute-start | bytes 5308424 | tf_op jit(solution)/shard_map/ppermute | solution.py:19
  7.0 42.0 %collective-permute-start = (bf16[384,3,768]{2,0,1:T(8,128)(2,1)}, bf16[384,3,768]{2,0,1:T(8,128)(2,1)}, u32[]{:S(2)}, u32[]{:S(2)}) collective-permute-start(bf16[384,3,768]{2,0,1:T(8,128)(2,1)} %param.12), channel_id=1, source_target_pairs={{0,28},{4,0},{8,4},{12,8},{16,12},{20,16},{24,20},{28,24},{1,29},{... | collective-permute-start | bytes 5308424 | tf_op jit(solution)/shard_map/ppermute | solution.py:21
  46.7 37.6 %collective-permute-start.3 = (bf16[384,3,768]{2,0,1:T(8,128)(2,1)S(1)}, bf16[384,3,768]{2,0,1:T(8,128)(2,1)}, u32[]{:S(2)}, u32[]{:S(2)}) collective-permute-start(bf16[384,3,768]{2,0,1:T(8,128)(2,1)S(1)} %collective-permute-done.1), channel_id=1, source_target_pairs={{0,4},{4,8},{8,12},{12,16},{16,20},{20,24},{24,28},{28,0},{1,5},{5... | collective-permute-start | bytes 5308424 | tf_op jit(solution)/shard_map/ppermute | solution.py:19
  48.1 36.2 %copy-start.8 = (s32[4]{0:T(128)}, s32[4]{0:T(128)S(1)}, u32[]{:S(2)}) copy-start(s32[4]{0:T(128)S(1)} %get-tuple-element.173) | copy-start | bytes 52
  49.0 44.0 %collective-permute-start.2 = (bf16[384,3,768]{2,0,1:T(8,128)(2,1)}, bf16[384,3,768]{2,0,1:T(8,128)(2,1)}, u32[]{:S(2)}, u32[]{:S(2)}) collective-permute-start(bf16[384,3,768]{2,0,1:T(8,128)(2,1)} %collective-permute-done), channel_id=1, source_target_pairs={{0,28},{4,0},{8,4},{12,8},{16,12},{20,16},{24,20},{28,24},{1,29},{... | collective-permute-start | bytes 5308424 | tf_op jit(solution)/shard_map/ppermute | solution.py:21
  84.3 34.9 %collective-permute-start.5 = (bf16[384,3,768]{2,0,1:T(8,128)(2,1)}, bf16[384,3,768]{2,0,1:T(8,128)(2,1)}, u32[]{:S(2)}, u32[]{:S(2)}) collective-permute-start(bf16[384,3,768]{2,0,1:T(8,128)(2,1)} %collective-permute-done.3), channel_id=1, source_target_pairs={{0,4},{4,8},{8,12},{12,16},{16,20},{20,24},{24,28},{28,0},{1,5},{5... | collective-permute-start | bytes 5308424 | tf_op jit(solution)/shard_map/ppermute | solution.py:19
  90.2 3.8 copy-start.4
  90.3 3.8 copy-start.6
  93.0 37.8 %collective-permute-start.4 = (bf16[384,3,768]{2,0,1:T(8,128)(2,1)}, bf16[384,3,768]{2,0,1:T(8,128)(2,1)S(1)}, u32[]{:S(2)}, u32[]{:S(2)}) collective-permute-start(bf16[384,3,768]{2,0,1:T(8,128)(2,1)} %collective-permute-done.2), channel_id=1, source_target_pairs={{0,28},{4,0},{8,4},{12,8},{16,12},{20,16},{24,20},{28,24},{1,29},{... | collective-permute-start | bytes 5308424 | tf_op jit(solution)/shard_map/ppermute | solution.py:21
  119.2 26.2 %collective-permute-start.6 = (bf16[384,3,768]{2,0,1:T(8,128)(2,1)}, bf16[384,3,768]{2,0,1:T(8,128)(2,1)S(1)}, u32[]{:S(2)}, u32[]{:S(2)}) collective-permute-start(bf16[384,3,768]{2,0,1:T(8,128)(2,1)} %collective-permute-done.5), channel_id=1, source_target_pairs={{0,4},{4,8},{8,12},{12,16},{16,20},{20,24},{24,28},{28,0},{1,5},{5... | collective-permute-start | bytes 5308424 | tf_op jit(solution)/shard_map/ppermute | solution.py:19
  146.5 1.5 copy-start
  148.1 0.8 copy-start.2
  148.1 0.8 copy-start.3
  148.4 2.9 copy-start.5
  148.4 3.1 copy-start.9
  148.5 3.2 copy-start.10
  148.5 3.3 copy-start.7
  150.6 396.9 %all-gather.5.cloned.1.call-start = ((), (), s32[]{:S(2)}) async-start(), calls=%async_computation.5 | async-start | bytes 5308416 | tf_op jit(solution)/shard_map/all_gather | solution.py:99
  259.7 6.3 %slice-start = ((s8[4718592]{0:T(1024)(128)(4,1)}), s8[4194304]{0:T(1024)(128)(4,1)S(1)}, s32[]{:S(2)}) async-start(s8[4718592]{0:T(1024)(128)(4,1)} %bitcast.157), calls=%async_computation.7 | async-start | bytes 8388608 | tf_op jit(solution)/shard_map/while
  262.2 3.9 slice-start.1
  283.8 6.3 %slice-start = ((s8[4718592]{0:T(1024)(128)(4,1)}), s8[4194304]{0:T(1024)(128)(4,1)S(1)}, s32[]{:S(2)}) async-start(s8[4718592]{0:T(1024)(128)(4,1)} %bitcast.157), calls=%async_computation.7 | async-start | bytes 8388608 | tf_op jit(solution)/shard_map/while
  286.2 3.9 slice-start.1
  307.9 6.3 %slice-start = ((s8[4718592]{0:T(1024)(128)(4,1)}), s8[4194304]{0:T(1024)(128)(4,1)S(1)}, s32[]{:S(2)}) async-start(s8[4718592]{0:T(1024)(128)(4,1)} %bitcast.157), calls=%async_computation.7 | async-start | bytes 8388608 | tf_op jit(solution)/shard_map/while
  310.3 3.9 slice-start.1
  332.0 6.3 %slice-start = ((s8[4718592]{0:T(1024)(128)(4,1)}), s8[4194304]{0:T(1024)(128)(4,1)S(1)}, s32[]{:S(2)}) async-start(s8[4718592]{0:T(1024)(128)(4,1)} %bitcast.157), calls=%async_computation.7 | async-start | bytes 8388608 | tf_op jit(solution)/shard_map/while
  334.4 3.9 slice-start.1
  356.0 6.3 %slice-start = ((s8[4718592]{0:T(1024)(128)(4,1)}), s8[4194304]{0:T(1024)(128)(4,1)S(1)}, s32[]{:S(2)}) async-start(s8[4718592]{0:T(1024)(128)(4,1)} %bitcast.157), calls=%async_computation.7 | async-start | bytes 8388608 | tf_op jit(solution)/shard_map/while
  358.4 3.9 slice-start.1
  380.1 6.3 %slice-start = ((s8[4718592]{0:T(1024)(128)(4,1)}), s8[4194304]{0:T(1024)(128)(4,1)S(1)}, s32[]{:S(2)}) async-start(s8[4718592]{0:T(1024)(128)(4,1)} %bitcast.157), calls=%async_computation.7 | async-start | bytes 8388608 | tf_op jit(solution)/shard_map/while
  382.5 3.9 slice-start.1
  404.1 6.3 %slice-start = ((s8[4718592]{0:T(1024)(128)(4,1)}), s8[4194304]{0:T(1024)(128)(4,1)S(1)}, s32[]{:S(2)}) async-start(s8[4718592]{0:T(1024)(128)(4,1)} %bitcast.157), calls=%async_computation.7 | async-start | bytes 8388608 | tf_op jit(solution)/shard_map/while
  406.5 3.9 slice-start.1
  428.2 6.3 %slice-start = ((s8[4718592]{0:T(1024)(128)(4,1)}), s8[4194304]{0:T(1024)(128)(4,1)S(1)}, s32[]{:S(2)}) async-start(s8[4718592]{0:T(1024)(128)(4,1)} %bitcast.157), calls=%async_computation.7 | async-start | bytes 8388608 | tf_op jit(solution)/shard_map/while
  430.6 3.9 slice-start.1
  448.7 18.9 %all-to-all-start.1 = ((f32[8,256,8]{1,2,0:T(8,128)}), f32[8,256,8]{1,2,0:T(8,128)S(1)}, u32[]{:S(2)}, u32[]{:S(2)}) async-start(f32[8,256,8]{1,2,0:T(8,128)} %bitcast.23), calls=%async_computation.1 | async-start | bytes 131072 | tf_op jit(solution)/shard_map/all_to_all | solution.py:175
  467.7 76.4 %all-to-all-start = ((f32[8,256,768]{1,2,0:T(8,128)}), f32[8,256,768]{1,2,0:T(8,128)}, u32[]{:S(2)}, u32[]{:S(2)}) async-start(f32[8,256,768]{1,2,0:T(8,128)} %copy.77), calls=%async_computation | async-start | bytes 12582912 | tf_op jit(solution)/shard_map/all_to_all | solution.py:176
  472.4 116.6 %reduce-scatter.2.cloned.1.call-start = ((), (), s32[]{:S(2)}) async-start(), calls=%async_computation.6 | async-start | bytes 1966080 | tf_op jit(solution)/shard_map/reduce_scatter | solution.py:193
Sparse Core Ops, SparseCore 0:
  150.7 39.0 all-gather.2
  191.7 38.9 all-gather.4
  552.6 36.4 reduce-scatter.1
